TPU v7x, 512 devices: a whole 4x8x8 slice. The times are simulated.
512 devices in a mesh: gx: 32 (over z, y_hi, core), gy: 16 (over x, y_lo).
Axes of the slice: x: 4, y: 8 (y_hi: 2, y_lo: 4; y = y_hi * 4 + y_lo), z: 8, core: 2. Of those that a mesh axis runs over, the one named last changes fastest.
Arguments:
- design: float32 [256, 128, 128], P('gx', 'gy'), may hold values from 0.06 to 0.9
- passive: int32 [256, 128, 128], P('gx', 'gy'), may hold values 0 or 1
- basis_pairs: float32 [4, 2, 3, 256, 128, 128], P(None, None, None, 'gx', 'gy'), may hold values from -6 to 6
- supports: int32 [256, 128, 128], P('gx', 'gy'), may hold values 0 or 1
- stiffness: float32 [24, 24], replicated, may hold values from -1.25 to 1.25
- mass_matrix: float32 [24, 24], replicated, may hold values from -1.25 to 1.25
- volume_fraction: float32 [64], replicated, may hold values from 0.26 to 0.36
Outputs:
- sensitivity: float32 [256, 128, 128], P('gx', 'gy')
- design_next: float32 [256, 128, 128], P('gx', 'gy')
All inputs are finite; a program needn't handle non-finite values. No bound on the sum of `passive` or of `supports` on one device may be relied on, other than what follows from the above.
Results may differ from a plain program's by a relative error of at most 0.0003.
Values sent between devices are 32-bit elements; how exact they have to be, the bound alone decides.
No kernel may reach another device: no remote copies, remote signals or barrier semaphores. Data moves between devices by JAX's collectives and lax.ppermute only.
A program may use at most 64 MiB of HBM per device.

v0:
```python
import math
import jax
import jax.numpy as jnp
from jax import lax
from jax.sharding import PartitionSpec as P

BISECT = 6
REGIONS = 64
PENALTY_SCALE = 3.0 * (1.0 - 0.001)
OMEGA_SQUARED = 0.5
MOVE_LIMIT = 0.2


def with_halo(cells, sides, width):
    for axis, dim in sides:
        count = lax.axis_size(axis)
        ends = count - 1
        head = lax.slice_in_dim(cells, 0, width, axis=dim)
        tail = lax.slice_in_dim(cells, cells.shape[dim] - width, cells.shape[dim], axis=dim)
        cells = jnp.concatenate(
            [
                lax.ppermute(tail, axis, [(i, (i + 1) % count) for i in range(ends)]),
                cells,
                lax.ppermute(head, axis, [((i + 1) % count, i) for i in range(ends)]),
            ],
            axis=dim,
        )
    return cells


def from_behind(value, axis, steps):
    count = lax.axis_size(axis)
    initial, last = (max(0, -steps), min(count, count - steps))
    return lax.ppermute(value, axis, [(source, source + steps) for source in range(initial, last)])


def filter_taps():
    tap_list = []
    for offset_x in range(-2, 3):
        for offset_y in range(-2, 3):
            for offset_z in range(-2, 3):
                weight = 3.0 - math.sqrt(
                    offset_x * offset_x + offset_y * offset_y + offset_z * offset_z
                )
                if weight > 0.0:
                    tap_list.append((offset_x, offset_y, offset_z, weight))
    return tap_list


def stencil(padded, block_shape):
    result = jnp.zeros(block_shape, jnp.float32)
    for offset_x, offset_y, offset_z, weight in filter_taps():
        result = (
            result
            + weight
            * padded[
                2 + offset_x : 2 + offset_x + block_shape[0],
                2 + offset_y : 2 + offset_y + block_shape[1],
                2 + offset_z : 2 + offset_z + block_shape[2],
            ]
        )
    return result


def element_terms(extended, stiffness, mass_matrix):
    pair_count = extended.shape[0]
    cells_x = extended.shape[3] - 1
    cells_y = extended.shape[4] - 1
    cells_z = extended.shape[5] - 1
    stiff_energy = jnp.zeros((cells_x * cells_y * cells_z,), jnp.float32)
    mass_energy = jnp.zeros((cells_x * cells_y * cells_z,), jnp.float32)
    for pair_index in range(pair_count):
        vectors = []
        for member in range(2):
            row_list = []
            for corner_x in (0, 1):
                for corner_y in (0, 1):
                    for corner_z in (0, 1):
                        for component in range(3):
                            row_list.append(
                                extended[
                                    pair_index,
                                    member,
                                    component,
                                    corner_x : corner_x + cells_x,
                                    corner_y : corner_y + cells_y,
                                    corner_z : corner_z + cells_z,
                                ].reshape(-1)
                            )
            vectors.append(jnp.stack(row_list))
        state_rows, adjoint_rows = vectors
        stiff_energy = stiff_energy + jnp.sum(
            state_rows * jnp.dot(stiffness, adjoint_rows, precision=lax.Precision.HIGHEST), axis=0
        )
        mass_energy = mass_energy + jnp.sum(
            state_rows * jnp.dot(mass_matrix, adjoint_rows, precision=lax.Precision.HIGHEST), axis=0
        )
    return (
        stiff_energy.reshape(cells_x, cells_y, cells_z),
        mass_energy.reshape(cells_x, cells_y, cells_z),
    )


def shards(design, passive, basis_pairs, supports, stiffness, mass_matrix, volume_fraction):
    block_shape = design.shape
    size_x, size_y, size_z = block_shape
    devices_x = lax.axis_size("gx")
    devices_y = lax.axis_size("gy")
    index_x = lax.axis_index("gx")
    index_y = lax.axis_index("gy")
    grid_x = size_x * devices_x
    grid_y = size_y * devices_y
    spread_x = jnp.arange(size_x + 4, dtype=jnp.int32) + index_x * size_x - 2
    spread_y = jnp.arange(size_y + 4, dtype=jnp.int32) + index_y * size_y - 2
    valid_x = ((spread_x >= 0) & (spread_x < grid_x)).astype(jnp.float32)
    valid_y = ((spread_y >= 0) & (spread_y < grid_y)).astype(jnp.float32)
    valid_z = jnp.pad(jnp.ones((size_z,), jnp.float32), 2)
    inside = valid_x[:, None, None] * valid_y[None, :, None] * valid_z[None, None, :]
    weight_sum = stencil(inside, block_shape)
    design_wide = with_halo(design, (("gx", 0), ("gy", 1)), 2)
    design_wide = jnp.pad(design_wide, ((0, 0), (0, 0), (2, 2)))
    physical = jnp.where(passive == 1, 1.0, stencil(design_wide, block_shape) / weight_sum)
    fields = basis_pairs * (1 - supports).astype(jnp.float32)
    rim_first = from_behind(fields[:, :, :, :1], "gx", -1)
    widened = jnp.concatenate([fields, rim_first], axis=3)
    rim_second = from_behind(widened[:, :, :, :, :1], "gy", -1)
    extended = jnp.concatenate([widened, rim_second], axis=4)
    extended = jnp.pad(extended, ((0, 0), (0, 0), (0, 0), (0, 0), (0, 0), (0, 1)))
    stiff_energy, mass_energy = element_terms(extended, stiffness, mass_matrix)
    raw_sensitivity = -(
        PENALTY_SCALE * physical * physical * stiff_energy - OMEGA_SQUARED * mass_energy
    )
    raw_sensitivity = jnp.where(passive == 1, 0.0, raw_sensitivity)
    scaled_wide = with_halo(raw_sensitivity / weight_sum, (("gx", 0), ("gy", 1)), 2)
    scaled_wide = jnp.pad(scaled_wide, ((0, 0), (0, 0), (2, 2)))
    sensitivity = stencil(scaled_wide, block_shape)
    benefit = jnp.maximum(-sensitivity, 0.0)
    floor_value = jnp.maximum(design - MOVE_LIMIT, 0.0)
    ceiling = jnp.minimum(design + MOVE_LIMIT, 1.0)
    band_cells = size_z // REGIONS
    target = volume_fraction * float(grid_x * grid_y * band_cells)

    def candidate(multiplier):
        per_cell = jnp.repeat(multiplier, band_cells)[None, None, :]
        trial = design * jnp.sqrt(benefit / per_cell)
        return jnp.where(passive == 1, 1.0, jnp.minimum(ceiling, jnp.maximum(floor_value, trial)))

    def region_sum(field):
        return jnp.sum(field, axis=(0, 1)).reshape(REGIONS, band_cells).sum(axis=1)

    levels = 1

    def bisect_round(round_index, bracket):
        low_end, high_end = bracket
        level_nodes = [(low_end, high_end)]
        midpoints = []
        next_nodes = []
        for node_low, node_high in level_nodes:
            middle = jnp.sqrt(node_low * node_high)
            midpoints.append(middle)
            next_nodes.append((node_low, middle))
            next_nodes.append((middle, node_high))
        partial_volumes = jnp.stack([region_sum(candidate(middle)) for middle in midpoints])
        volumes = lax.psum(partial_volumes, ("gx", "gy"))
        position = jnp.zeros((REGIONS,), jnp.int32)
        middle = jnp.sqrt(low_end * high_end)
        heap_index = position + (2**0 - 1)
        chosen = jnp.take_along_axis(volumes, heap_index[None, :], axis=0)[0]
        heavier = chosen > target
        low_end = jnp.where(heavier, middle, low_end)
        high_end = jnp.where(heavier, high_end, middle)
        return (low_end, high_end)

    start = (jnp.full((REGIONS,), 0.0001, jnp.float32), jnp.full((REGIONS,), 10000.0, jnp.float32))
    low_end, high_end = lax.fori_loop(0, BISECT // levels, bisect_round, start)
    design_next = candidate(jnp.sqrt(low_end * high_end))
    return (sensitivity, design_next)


def solution(mesh):
    placed = (
        P("gx", "gy", None),
        P("gx", "gy", None),
        P(None, None, None, "gx", "gy", None),
        P("gx", "gy", None),
        P(),
        P(),
        P(),
    )
    return jax.shard_map(
        shards,
        mesh=mesh,
        in_specs=placed,
        out_specs=(P("gx", "gy", None), P("gx", "gy", None)),
        check_vma=False,
    )
```

profile of v0, /device:TPU:1, one launch (start us, length us, event | category | flops | bytes accessed | tf_op | source)
XLA Modules:
  0.0 711.6 jit_solution(10859632898439551738)
XLA Ops:
  1.4 8.8 %collective-permute-start.1 = (f32[2,8,128]{2,1,0:T(8,128)S(1)}, f32[2,8,128]{2,1,0:T(8,128)S(1)}, u32[]{:S(2)}, u32[]{:S(2)}) collective-permute-start(f32[2,8,128]{2,1,0:T(8,128)S(1)} %get-tuple-element.311), channel_id=1, source_target_pairs={{16,0},{32,16},{48,32},{64,48},{80,64},{96,80},{112,96},{128,112},... | collective-permute-start | bytes 24584 | tf_op jit(solution)/shard_map/ppermute | solution.py:24
  21.3 3.0 collective-permute-done.3
  28.6 5.1 collective-permute-done.5
  39.8 3.7 stack.27
  43.5 5.8 stack.28
  49.3 2.7 fusion.12
  53.5 3.7 stack.34
  57.2 5.8 stack.33
  63.0 2.7 fusion.15
  69.2 3.6 stack.30
  73.0 3.6 stack.29
  78.7 3.4 stack.32
  82.1 3.4 stack.31
  88.7 8.4 %collective-permute-start.6 = (f32[2,8,128]{2,1,0:T(8,128)S(1)}, f32[2,8,128]{2,1,0:T(8,128)S(1)}, u32[]{:S(2)}, u32[]{:S(2)}) collective-permute-start(f32[2,8,128]{2,1,0:T(8,128)S(1)} %get-tuple-element.309), channel_id=1, source_target_pairs={{0,16},{16,32},{32,48},{48,64},{64,80},{80,96},{96,112},{112,128},... | collective-permute-start | bytes 24584 | tf_op jit(solution)/shard_map/ppermute | solution.py:22
  99.0 6.9 collective-permute-done.7
  106.0 2.8 collective-permute-start.8
  110.1 5.8 collective-permute-done.9
  116.6 594.0 %while.13 = (s32[]{:T(128)}, f32[64]{0:T(128)S(1)}, f32[64]{0:T(128)S(1)}, s32[8,8,128]{2,1,0:T(8,128)S(1)}, f32[8,8,128]{2,1,0:T(8,128)S(1)}, /*index=5*/f32[8,...) while((s32[]{:T(128)}, f32[64]{0:T(128)S(1)}, ...), condition=%wide.region_12.13_spmd.clone, body=%wide.region_8.12_spmd.clone.sunk | while | flops 57923 | bytes 172676 | solution.py:175
  117.2 111.4 %psum.9 = f32[1,64]{1,0:T(1,128)S(1)} all-reduce(f32[1,64]{1,0:T(1,128)S(1)} %bitcast.455), channel_id=1, replica_groups=mesh['gx'=32,'gy'=16] {'gx','gy'}, use_global_device_ids=true, to_apply=%region_11.11 | all-reduce | flops 64 | bytes 512 | tf_op jit(solution)/shard_map/while/body/eval_jaxpr/psum | solution.py:164
  230.0 95.1 %psum.9 = f32[1,64]{1,0:T(1,128)S(1)} all-reduce(f32[1,64]{1,0:T(1,128)S(1)} %bitcast.455), channel_id=1, replica_groups=mesh['gx'=32,'gy'=16] {'gx','gy'}, use_global_device_ids=true, to_apply=%region_11.11 | all-reduce | flops 64 | bytes 512 | tf_op jit(solution)/shard_map/while/body/eval_jaxpr/psum | solution.py:164
  326.4 94.7 %psum.9 = f32[1,64]{1,0:T(1,128)S(1)} all-reduce(f32[1,64]{1,0:T(1,128)S(1)} %bitcast.455), channel_id=1, replica_groups=mesh['gx'=32,'gy'=16] {'gx','gy'}, use_global_device_ids=true, to_apply=%region_11.11 | all-reduce | flops 64 | bytes 512 | tf_op jit(solution)/shard_map/while/body/eval_jaxpr/psum | solution.py:164
  422.4 95.0 %psum.9 = f32[1,64]{1,0:T(1,128)S(1)} all-reduce(f32[1,64]{1,0:T(1,128)S(1)} %bitcast.455), channel_id=1, replica_groups=mesh['gx'=32,'gy'=16] {'gx','gy'}, use_global_device_ids=true, to_apply=%region_11.11 | all-reduce | flops 64 | bytes 512 | tf_op jit(solution)/shard_map/while/body/eval_jaxpr/psum | solution.py:164
  518.8 94.7 %psum.9 = f32[1,64]{1,0:T(1,128)S(1)} all-reduce(f32[1,64]{1,0:T(1,128)S(1)} %bitcast.455), channel_id=1, replica_groups=mesh['gx'=32,'gy'=16] {'gx','gy'}, use_global_device_ids=true, to_apply=%region_11.11 | all-reduce | flops 64 | bytes 512 | tf_op jit(solution)/shard_map/while/body/eval_jaxpr/psum | solution.py:164
  614.9 95.0 %psum.9 = f32[1,64]{1,0:T(1,128)S(1)} all-reduce(f32[1,64]{1,0:T(1,128)S(1)} %bitcast.455), channel_id=1, replica_groups=mesh['gx'=32,'gy'=16] {'gx','gy'}, use_global_device_ids=true, to_apply=%region_11.11 | all-reduce | flops 64 | bytes 512 | tf_op jit(solution)/shard_map/while/body/eval_jaxpr/psum | solution.py:164
  (232 shorter events, 44.2 us)
Async XLA Ops:
  0.6 48.7 %copy-start = (f32[24,24]{1,0:T(8,128)S(1)}, f32[24,24]{1,0:T(8,128)}, u32[]{:S(2)}) copy-start(f32[24,24]{1,0:T(8,128)} %param.14) | copy-start | bytes 6916
  0.6 16.8 %copy-start.3 = (f32[8,8,128]{2,1,0:T(8,128)S(1)}, f32[8,8,128]{2,1,0:T(8,128)}, u32[]{:S(2)}) copy-start(f32[8,8,128]{2,1,0:T(8,128)} %param.9) | copy-start | bytes 98308
  1.4 16.1 %collective-permute-start.1 = (f32[2,8,128]{2,1,0:T(8,128)S(1)}, f32[2,8,128]{2,1,0:T(8,128)S(1)}, u32[]{:S(2)}, u32[]{:S(2)}) collective-permute-start(f32[2,8,128]{2,1,0:T(8,128)S(1)} %get-tuple-element.311), channel_id=1, source_target_pairs={{16,0},{32,16},{48,32},{64,48},{80,64},{96,80},{112,96},{128,112},... | collective-permute-start | bytes 24584 | tf_op jit(solution)/shard_map/ppermute | solution.py:24
  10.2 7.3 %collective-permute-start = (f32[2,8,128]{2,1,0:T(8,128)S(1)}, f32[2,8,128]{2,1,0:T(8,128)S(1)}, u32[]{:S(2)}, u32[]{:S(2)}) collective-permute-start(f32[2,8,128]{2,1,0:T(8,128)S(1)} %get-tuple-element.312), channel_id=1, source_target_pairs={{0,16},{16,32},{32,48},{48,64},{64,80},{80,96},{96,112},{112,128},... | collective-permute-start | bytes 24584 | tf_op jit(solution)/shard_map/ppermute | solution.py:22
  14.2 10.3 %collective-permute-start.4 = (f32[4,2,3,1,8,128]{5,4,3,2,1,0:T(8,128)S(1)}, f32[4,2,3,1,8,128]{5,4,3,2,1,0:T(8,128)S(1)}, u32[]{:S(2)}, u32[]{:S(2)}) collective-permute-start(f32[4,2,3,1,8,128]{5,4,3,2,1,0:T(8,128)S(1)} %slice.2402), channel_id=1, source_target_pairs={{16,0},{32,16},{48,32},{64,48},{80,64},{96,80},{112,96},{128,112},... | collective-permute-start | bytes 294920 | tf_op jit(solution)/shard_map/ppermute | solution.py:34
  17.5 3.7 collective-permute-start.2
  19.9 4.5 collective-permute-start.3
  25.0 8.7 %collective-permute-start.5 = (f32[4,2,3,9,1,128]{5,3,4,2,1,0:T(8,128)S(1)}, f32[4,2,3,9,1,128]{5,3,4,2,1,0:T(8,128)S(1)}, u32[]{:S(2)}, u32[]{:S(2)}) collective-permute-start(f32[4,2,3,9,1,128]{5,3,4,2,1,0:T(8,128)S(1)} %copy.107), channel_id=1, source_target_pairs={{1,0},{2,1},{3,2},{4,3},{5,4},{6,5},{7,6},{8,7},{9,8},{10,9},{11,1... | collective-permute-start | bytes 331784 | tf_op jit(solution)/shard_map/ppermute | solution.py:34
  43.5 8.5 %copy-start.5 = (f32[24,24]{1,0:T(8,128)S(1)}, f32[24,24]{1,0:T(8,128)}, u32[]{:S(2)}) copy-start(f32[24,24]{1,0:T(8,128)} %param.13) | copy-start | bytes 6916
  68.1 4.8 copy-start.15
  68.1 4.8 copy-start.16
  68.1 4.8 copy-start.17
  68.1 4.8 copy-start.18
  68.1 4.8 copy-start.19
  68.1 4.8 copy-start.20
  68.1 4.8 copy-start.21
  68.1 4.8 copy-start.22
  68.1 4.8 copy-start.23
  87.4 22.6 %copy-start.57 = (f32[64]{0:T(128)S(1)}, f32[64]{0:T(128)}, u32[]{:S(2)}) copy-start(f32[64]{0:T(128)} %param.15) | copy-start | bytes 772
  88.7 10.3 %collective-permute-start.6 = (f32[2,8,128]{2,1,0:T(8,128)S(1)}, f32[2,8,128]{2,1,0:T(8,128)S(1)}, u32[]{:S(2)}, u32[]{:S(2)}) collective-permute-start(f32[2,8,128]{2,1,0:T(8,128)S(1)} %get-tuple-element.309), channel_id=1, source_target_pairs={{0,16},{16,32},{32,48},{48,64},{64,80},{80,96},{96,112},{112,128},... | collective-permute-start | bytes 24584 | tf_op jit(solution)/shard_map/ppermute | solution.py:22
  97.1 8.9 %collective-permute-start.7 = (f32[2,8,128]{2,1,0:T(8,128)S(1)}, f32[2,8,128]{2,1,0:T(8,128)S(1)}, u32[]{:S(2)}, u32[]{:S(2)}) collective-permute-start(f32[2,8,128]{2,1,0:T(8,128)S(1)} %get-tuple-element.310), channel_id=1, source_target_pairs={{16,0},{32,16},{48,32},{64,48},{80,64},{96,80},{112,96},{128,112},... | collective-permute-start | bytes 24584 | tf_op jit(solution)/shard_map/ppermute | solution.py:24
  106.0 4.1 collective-permute-start.8
  108.7 7.1 %collective-permute-start.9 = (f32[12,2,128]{2,1,0:T(2,128)S(1)}, f32[12,2,128]{2,1,0:T(2,128)S(1)}, u32[]{:S(2)}, u32[]{:S(2)}) collective-permute-start(f32[12,2,128]{2,1,0:T(2,128)S(1)} %get-tuple-element.301), channel_id=1, source_target_pairs={{1,0},{2,1},{3,2},{4,3},{5,4},{6,5},{7,6},{8,7},{9,8},{10,9},{11,1... | collective-permute-start | bytes 36872 | tf_op jit(solution)/shard_map/ppermute | solution.py:24
  116.6 594.3 %copy-start.33 = (f32[8,8,128]{2,1,0:T(8,128)}, f32[8,8,128]{2,1,0:T(8,128)S(1)}, u32[]{:S(2)}) copy-start(f32[8,8,128]{2,1,0:T(8,128)S(1)} %get-tuple-element.101) | copy-start | bytes 98308
  (44 other events, 120.5 us)
where the time goes:
time: 714 us; the launch traced here: 712 us
  blocking collectives  586 us (82%)
  local copies, waits for them, and re-layouts  50.1 us (7%)
  starting transfers between devices  32.4 us (5%)
  waiting for transfers between devices  20.9 us (3%)
  matrix products  11.6 us (2%)
  other arithmetic  8.48 us (1%)
    psum x6, blocking collectives, bisect_round(): volumes = lax.psum(partial_volumes, ('gx', 'gy'))  586 us
    another operation x8, local copies, waits for them, and re-layouts, element_terms(): vectors.append(jnp.stack(row_list))  33.2 us
    ppermute x4, waiting for transfers between devices, with_halo(): lax.ppermute(head, axis, [((i + 1) % count, i) for i in range(ends)])  15.8 us
    ppermute x4, starting transfers between devices, with_halo(): lax.ppermute(tail, axis, [(i, (i + 1) % count) for i in range(ends)])  15.5 us
  transfers between devices with their start and end apart: 10, of which 4 were waited for; matrix products, arithmetic and copies ran while one was open for 1% of the time, Pallas kernels for 0%

commit v1 on v0

--- a/solution.py
+++ b/solution.py
@@ -161,7 +161,8 @@
             next_nodes.append((node_low, middle))
             next_nodes.append((middle, node_high))
         partial_volumes = jnp.stack([region_sum(candidate(middle)) for middle in midpoints])
-        volumes = lax.psum(partial_volumes, ("gx", "gy"))
+        parts = lax.all_gather(partial_volumes, ("gx", "gy"), axis=0, tiled=False)
+        volumes = parts.sum(axis=0)
         position = jnp.zeros((REGIONS,), jnp.int32)
         middle = jnp.sqrt(low_end * high_end)
         heap_index = position + (2**0 - 1)

time: 714 us -> 1730 us (2.42)
  waiting for transfers between devices: 20.9 us -> 1590 us
  blocking collectives: 586 us -> 0 us
    while x0 -> x12, waiting for transfers between devices: none -> 1570 us
    psum x6 -> x0, blocking collectives: 586 us -> none  [bisect_round(): volumes = lax.psum(partial_volumes, ('gx', 'gy'))]
  transfers between devices with their start and end apart: 10 -> 16, of which waited for: 4 -> 10; matrix products, arithmetic and copies ran while one was open for 1% -> 0% of each run, Pallas kernels for 0% -> 0%
where the time goes in v1:
time: 1730 us
  waiting for transfers between devices  1590 us (92%)
  local copies, waits for them, and re-layouts  61.6 us (4%)
  starting transfers between devices  32.6 us (2%)
    while x12, waiting for transfers between devices  1570 us
  transfers between devices with their start and end apart: 16, of which 10 were waited for; matrix products, arithmetic and copies ran while one was open for 0% of the time, Pallas kernels for 0%

profile of v1, /device:TPU:1, one launch (start us, length us, event | category | flops | bytes accessed | tf_op | source)
XLA Modules:
  0.0 1725.4 jit_solution(15887802011969009662)
XLA Ops:
  8.0 8.8 collective-permute-start.1
  27.8 3.0 collective-permute-done.3
  35.1 5.2 collective-permute-done.5
  46.2 3.7 stack.27
  49.9 5.8 stack.28
  55.8 2.7 fusion.12
  59.9 3.7 stack.34
  63.6 5.8 stack.33
  69.4 2.7 fusion.15
  75.4 3.6 stack.30
  79.3 3.6 stack.29
  84.9 3.4 stack.32
  88.4 3.4 stack.31
  95.0 8.4 collective-permute-start.6
  105.3 6.9 collective-permute-done.7
  112.3 2.8 collective-permute-start.8
  116.4 5.8 collective-permute-done.9
  122.9 1594.7 %while.13 = (s32[]{:T(128)}, f32[64]{0:T(128)S(1)}, f32[64]{0:T(128)S(1)}, s32[8,8,128]{2,1,0:T(8,128)S(1)}, f32[8,8,128]{2,1,0:T(8,128)S(1)}, /*index=5*/f32[8,...) while((s32[]{:T(128)}, f32[64]{0:T(128)S(1)}, ...), condition=%wide.region_12.13_spmd.clone, body=%wide.region_8.12_spmd.clone.sunk | while | flops 123334 | bytes 2008072 | solution.py:176
  124.5 277.1 %all-reduce.10.cloned.1.call-done = f32[32768]{0:T(1024)} async-done(((f32[32768]{0:T(1024)}), f32[32768]{0:T(1024)}) %all-reduce.10.cloned.1.call-update) | async-done | bytes 131088 | tf_op jit(solution)/shard_map/while
  405.1 259.5 %all-reduce.10.cloned.1.call-done = f32[32768]{0:T(1024)} async-done(((f32[32768]{0:T(1024)}), f32[32768]{0:T(1024)}) %all-reduce.10.cloned.1.call-update) | async-done | bytes 131088 | tf_op jit(solution)/shard_map/while
  668.1 259.5 %all-reduce.10.cloned.1.call-done = f32[32768]{0:T(1024)} async-done(((f32[32768]{0:T(1024)}), f32[32768]{0:T(1024)}) %all-reduce.10.cloned.1.call-update) | async-done | bytes 131088 | tf_op jit(solution)/shard_map/while
  931.1 259.2 %all-reduce.10.cloned.1.call-done = f32[32768]{0:T(1024)} async-done(((f32[32768]{0:T(1024)}), f32[32768]{0:T(1024)}) %all-reduce.10.cloned.1.call-update) | async-done | bytes 131088 | tf_op jit(solution)/shard_map/while
  1193.8 259.2 %all-reduce.10.cloned.1.call-done = f32[32768]{0:T(1024)} async-done(((f32[32768]{0:T(1024)}), f32[32768]{0:T(1024)}) %all-reduce.10.cloned.1.call-update) | async-done | bytes 131088 | tf_op jit(solution)/shard_map/while
  1456.5 259.2 %all-reduce.10.cloned.1.call-done = f32[32768]{0:T(1024)} async-done(((f32[32768]{0:T(1024)}), f32[32768]{0:T(1024)}) %all-reduce.10.cloned.1.call-update) | async-done | bytes 131088 | tf_op jit(solution)/shard_map/while
  (280 shorter events, 56.4 us)
Async XLA Ops:
  7.2 48.6 %copy-start = (f32[24,24]{1,0:T(8,128)S(1)}, f32[24,24]{1,0:T(8,128)}, u32[]{:S(2)}) copy-start(f32[24,24]{1,0:T(8,128)} %param.14) | copy-start | bytes 6916
  7.2 16.8 copy-start.4
  8.0 16.1 collective-permute-start.1
  16.7 7.3 collective-permute-start
  20.7 10.3 collective-permute-start.4
  24.1 3.7 collective-permute-start.2
  26.4 4.5 collective-permute-start.3
  31.5 8.7 collective-permute-start.5
  49.9 8.5 copy-start.6
  74.4 4.8 copy-start.16
  74.4 4.8 copy-start.17
  74.4 4.8 copy-start.18
  93.7 22.6 %copy-start.58 = (f32[64]{0:T(128)S(1)}, f32[64]{0:T(128)}, u32[]{:S(2)}) copy-start(f32[64]{0:T(128)} %param.15) | copy-start | bytes 772
  95.0 10.3 collective-permute-start.6
  103.4 8.9 collective-permute-start.7
  112.3 4.1 collective-permute-start.8
  115.0 7.1 collective-permute-start.9
  122.9 1595.0 %copy-start.34 = (f32[8,8,128]{2,1,0:T(8,128)}, f32[8,8,128]{2,1,0:T(8,128)S(1)}, u32[]{:S(2)}) copy-start(f32[8,8,128]{2,1,0:T(8,128)S(1)} %get-tuple-element.101) | copy-start | bytes 98308
  123.0 278.7 %all-reduce.10.cloned.1.call-start = ((), (), s32[]{:S(2)}) async-start(), calls=%async_computation | async-start | bytes 262144 | tf_op jit(solution)/shard_map/while
  403.6 261.1 %all-reduce.10.cloned.1.call-start = ((), (), s32[]{:S(2)}) async-start(), calls=%async_computation | async-start | bytes 262144 | tf_op jit(solution)/shard_map/while
  666.6 261.1 %all-reduce.10.cloned.1.call-start = ((), (), s32[]{:S(2)}) async-start(), calls=%async_computation | async-start | bytes 262144 | tf_op jit(solution)/shard_map/while
  929.6 260.8 %all-reduce.10.cloned.1.call-start = ((), (), s32[]{:S(2)}) async-start(), calls=%async_computation | async-start | bytes 262144 | tf_op jit(solution)/shard_map/while
  1192.3 260.8 %all-reduce.10.cloned.1.call-start = ((), (), s32[]{:S(2)}) async-start(), calls=%async_computation | async-start | bytes 262144 | tf_op jit(solution)/shard_map/while
  1455.0 260.8 %all-reduce.10.cloned.1.call-start = ((), (), s32[]{:S(2)}) async-start(), calls=%async_computation | async-start | bytes 262144 | tf_op jit(solution)/shard_map/while
  (56 other events, 152.6 us)
Sparse Core Ops, SparseCore 0:
  128.8 272.8 all-reduce.9
  409.4 255.2 all-reduce.9
  672.4 255.2 all-reduce.9
  935.1 255.2 all-reduce.9
  1197.8 255.2 all-reduce.9
  1460.5 255.2 all-reduce.9
